TPU v7x, 512 devices: a whole 4x8x8 slice. The times are simulated.
512 devices in a mesh: rep: 32 (over x, z), tp: 16 (over y, core).
Axes of the slice: x: 4, y: 8, z: 8, core: 2. Of those that a mesh axis runs over, the one named last changes fastest.
Arguments:
- queries: bfloat16 [10240, 8192], P('rep', 'tp'), may hold values from -30 to 30
- fresh_kv: bfloat16 [10240, 4096], P('rep', 'tp'), may hold values from -6 to 6, as said below
- kv_cache: bfloat16 [1408, 16, 8, 256], P('rep', 'tp'), may hold values from -6 to 6, as said below
- cached_len: int32 [640], P('rep'), may hold values from 1 to 48, as said below
- page_table: int32 [640, 6], P('rep'), may hold values from 0 to 43, as said below
- out_weight: bfloat16 [8192, 4096], P('tp'), may hold values from -0.09375 to 0.09375
- adapter_down: bfloat16 [64, 64, 8192], P('rep', None, 'tp'), may hold values from -0.0625 to 0.0625
- pooled_up_weight: bfloat16 [64, 64, 4096], P('rep', None, 'tp'), may hold values from -0.75 to 0.75
- adapter_ids: int32 [640], P('rep'), may hold values from 0 to 63, as said below
- pool_slot: int32 [64], replicated, may hold values from 0 to 63, as said below
Outputs:
- adapted_output: bfloat16 [10240, 4096], P('rep', 'tp')
Inputs may be any that keep to these rules, and one draw needn't show every extreme that they name: `kv_cache`: slots that hold the same key-value head are equal. `fresh_kv`: slots that hold the same key-value head are equal. `cached_len`: A row with cached length n uses its first ceil(n / 8) page table entries; in every replica some row has 48. `page_table`: entries index the 44 pages of the row's own replica. The pages that a row uses are distinct, no page is used by two rows of one replica, every page of a replica is used, and entries past a row's used pages repeat its first page. `adapter_ids`: row r of replica i is entry i * 20 + r. The owner of adapter a is replica pool_slot[a] // 2. Within one replica at most 2 rows name adapters of one owner, and one owner, the same for all replicas, is named by exactly 2 rows of every replica. A permutation: adapter a's blocks are adapter_down[pool_slot[a]] and pooled_up_weight[pool_slot[a]].
All inputs are finite; a program needn't handle non-finite values.
Results may differ from a plain program's by a relative error of at most 0.023.
Values may be sent and summed in bfloat16 or wider, within the bound.
No kernel may reach another device: no remote copies, remote signals or barrier semaphores. Data moves between devices by JAX's collectives and lax.ppermute only.
A program may use at most 64 MiB of HBM per device.

v0:
```python
import math

import jax
import jax.numpy as jnp
from jax import lax
from jax.sharding import PartitionSpec as P

ADAPTER_SCALE = 2.0


def shards(
    queries,
    fresh_kv,
    kv_cache,
    cached_len,
    page_table,
    out_weight,
    adapter_down,
    pooled_up_weight,
    adapter_ids,
    pool_slot,
):
    row_count = cached_len.shape[0]
    token_count = queries.shape[0]
    per_row = token_count // row_count
    slot_count = kv_cache.shape[1]
    page_len = kv_cache.shape[2]
    head_dim = kv_cache.shape[3] // 2
    feat_width = queries.shape[1]
    head_count = feat_width // head_dim
    heads_per_slot = head_count // slot_count
    cache_span = page_table.shape[1] * page_len
    output_columns = pooled_up_weight.shape[2]
    rank_size = adapter_down.shape[1]
    paged_kv = (
        kv_cache[page_table]
        .transpose(0, 2, 1, 3, 4)
        .reshape(row_count, slot_count, cache_span, 2 * head_dim)
    )
    recent = fresh_kv.reshape(row_count, per_row, slot_count, 2 * head_dim).transpose(0, 2, 1, 3)
    entries = jnp.concatenate([paged_kv, recent], axis=2)
    key_part = entries[..., :head_dim]
    value_part = entries[..., head_dim:]
    query_rows = queries.reshape(
        row_count, per_row, slot_count, heads_per_slot, head_dim
    ).transpose(0, 2, 1, 3, 4)
    query_rows = query_rows.reshape(row_count, slot_count, per_row * heads_per_slot, head_dim)
    scores = jnp.einsum(
        "rsad,rskd->rsak", query_rows, key_part, preferred_element_type=jnp.float32
    ) / math.sqrt(head_dim)
    entry_ids = jnp.arange(cache_span + per_row)[None, None, None, :]
    token_ids = (jnp.arange(per_row * heads_per_slot) // heads_per_slot)[None, None, :, None]
    allowed = jnp.where(
        entry_ids < cache_span,
        entry_ids < cached_len[:, None, None, None],
        entry_ids - cache_span <= token_ids,
    )
    scores = jnp.where(allowed, scores, -jnp.inf)
    peak_score = jnp.max(scores, axis=-1, keepdims=True)
    raised = jnp.exp(scores - peak_score)
    weights = (raised / jnp.sum(raised, axis=-1, keepdims=True)).astype(jnp.bfloat16)
    attended = jnp.einsum(
        "rsak,rskd->rsad", weights, value_part, preferred_element_type=jnp.float32
    ).astype(jnp.bfloat16)
    attended = attended.reshape(row_count, slot_count, per_row, heads_per_slot, head_dim).transpose(
        0, 2, 1, 3, 4
    )
    attended = attended.reshape(token_count, feat_width)
    plain_output = (
        lax.psum_scatter(
            lax.dot_general(
                out_weight, attended, (((0,), (1,)), ((), ())), preferred_element_type=jnp.float32
            ).astype(jnp.bfloat16),
            "tp",
            scatter_dimension=0,
            tiled=True,
        )
        .astype(jnp.float32)
        .T
    )
    slot_hits = adapter_ids[:, None] == jnp.arange(pool_slot.shape[0])[None, :]
    pool_position = jnp.sum(jnp.where(slot_hits, pool_slot[None, :], 0), axis=1)
    by_row = attended.reshape(row_count, per_row, feat_width)
    replicas = lax.axis_size("rep")
    local_count = adapter_down.shape[0]
    capacity = (row_count + replicas - 1) // replicas + 1
    owner_of = pool_position // local_count
    local_slot = pool_position % local_count
    same_owner = owner_of[:, None] == owner_of[None, :]
    earlier = jnp.arange(row_count)[None, :] < jnp.arange(row_count)[:, None]
    seat_of = jnp.sum(same_owner & earlier, axis=1)
    target = owner_of * capacity + seat_of
    placing = jnp.arange(replicas * capacity)[:, None] == target[None, :]
    placing_mat = placing.astype(jnp.bfloat16)
    wanted = (jnp.sum(jnp.where(placing, local_slot[None, :] + 1, 0), axis=1) - 1).reshape(
        replicas, capacity
    )
    choose = (
        lax.all_to_all(wanted, "rep", split_axis=0, concat_axis=0, tiled=True)[:, :, None]
        == jnp.arange(local_count)[None, None, :]
    ).astype(jnp.bfloat16)
    down_blocks = jnp.einsum(
        "smj,jkf->smkf", choose, adapter_down, preferred_element_type=jnp.float32
    ).astype(jnp.bfloat16)
    up_blocks = jnp.einsum(
        "smj,jkd->smkd", choose, pooled_up_weight, preferred_element_type=jnp.float32
    ).astype(jnp.bfloat16)
    down_got = lax.all_to_all(down_blocks, "rep", split_axis=0, concat_axis=0, tiled=True)
    up_got = lax.all_to_all(up_blocks, "rep", split_axis=0, concat_axis=0, tiled=True)
    down_got = down_got.reshape(replicas * capacity, rank_size, feat_width)
    up_got = up_got.reshape(replicas * capacity, rank_size, output_columns)
    down_sel = jnp.einsum(
        "sr,skf->rkf", placing_mat, down_got, preferred_element_type=jnp.float32
    ).astype(jnp.bfloat16)
    up_sel = jnp.einsum(
        "sr,skd->rkd", placing_mat, up_got, preferred_element_type=jnp.float32
    ).astype(jnp.bfloat16)
    shrink_part = jnp.einsum("rqf,rkf->rqk", by_row, down_sel, preferred_element_type=jnp.float32)
    down_projected = lax.psum(shrink_part.astype(jnp.bfloat16), "tp")
    adapter_correction = jnp.einsum(
        "owe,oet->owt", down_projected, up_sel, preferred_element_type=jnp.float32
    ).astype(jnp.bfloat16)
    adapted_output = plain_output + ADAPTER_SCALE * adapter_correction.reshape(
        token_count, output_columns
    ).astype(jnp.float32)
    return adapted_output.astype(jnp.bfloat16)


def solution(mesh):
    return jax.shard_map(
        shards,
        mesh=mesh,
        in_specs=(
            P("rep", "tp"),
            P("rep", "tp"),
            P("rep", "tp", None, None),
            P("rep"),
            P("rep", None),
            P("tp", None),
            P("rep", None, "tp"),
            P("rep", None, "tp"),
            P("rep"),
            P(),
        ),
        out_specs=P("rep", "tp"),
        check_vma=False,
    )
```

profile of v0, /device:TPU:1, one launch (start us, length us, event | category | flops | bytes accessed | tf_op | source)
XLA Modules:
  0.0 252.2 jit_solution(10275384888598889129)
XLA Ops:
  6.5 0.0 copy-start
  6.5 0.9 select_reduce_fusion.1
  7.4 0.2 convert_reduce_fusion
  7.6 0.1 select_reduce_fusion
  7.7 0.1 sub.34
  7.8 22.2 %all_to_all.16 = s32[32,1,2]{2,1,0:T(1,128)S(1)} all-to-all(s32[32,1,2]{2,1,0:T(1,128)S(1)} %bitcast.62), channel_id=1, replica_groups=mesh['rep'=32,'tp'=16] {'rep'}, dimensions={0} | all-to-all | bytes 512 | tf_op jit(solution)/shard_map/all_to_all | solution.py:99
  30.0 0.1 copy.38
  30.1 1.6 convolution_convert_fusion.2
  31.7 2.5 copy.44
  34.2 0.0 copy-start.2
  34.2 4.1 %all-to-all-start.2 = ((bf16[32,2,64,256]{3,2,1,0:T(8,128)(2,1)}), bf16[32,2,64,256]{3,2,1,0:T(8,128)(2,1)S(1)}, u32[]{:S(2)}, u32[]{:S(2)}) async-start(bf16[32,2,64,256]{3,2,1,0:T(8,128)(2,1)} %copy.44), calls=%async_computation.3 | async-start | bytes 4194304 | tf_op jit(solution)/shard_map/all_to_all | solution.py:109
  38.4 0.0 copy-done.2
  38.4 1.3 convolution_convert_fusion.1
  39.7 4.3 %copy.40 = bf16[32,2,64,512]{3,2,1,0:T(8,128)(2,1)} copy(bf16[32,2,64,512]{3,0,2,1:T(8,128)(2,1)S(1)} %convolution_convert_fusion.1) | data formatting | bytes 8388608 | tf_op jit(solution)/shard_map/convert_element_type | solution.py:104
  44.0 0.0 copy-start.3
  44.0 0.0 copy-start.1
  44.0 0.0 copy-start.4
  44.0 0.0 copy-start.5
  44.0 43.8 %all-to-all-done.2 = bf16[32,2,64,256]{3,2,1,0:T(8,128)(2,1)S(1)} async-done(((bf16[32,2,64,256]{3,2,1,0:T(8,128)(2,1)}), bf16[32,2,64,256]{3,2,1,0:T(8,128)(2,1)S(1)}, u32[]{:S(2)}, u32[]{:S(2)}) %all-to-all-start.2) | async-done | bytes 2097184 | tf_op jit(solution)/shard_map/all_to_all | solution.py:109
  87.8 6.2 %all-to-all-start.1 = ((bf16[32,2,64,512]{3,2,1,0:T(8,128)(2,1)}), bf16[32,2,64,512]{3,2,1,0:T(8,128)(2,1)}, u32[]{:S(2)}, u32[]{:S(2)}) async-start(bf16[32,2,64,512]{3,2,1,0:T(8,128)(2,1)} %copy.40), calls=%async_computation.2 | async-start | bytes 8388608 | tf_op jit(solution)/shard_map/all_to_all | solution.py:108
  94.0 0.2 reduce-scatter.2.cloned.1.call-start
  94.3 0.0 copy-done.3
  94.3 0.1 copy.35
  94.4 0.1 reshape.210
  94.5 0.0 copy-done.1
  94.5 0.2 reshape.202
  94.7 0.0 copy-done
  94.7 0.7 gather_fusion
  95.4 0.0 copy-done.4
  95.4 0.1 iota_compare_fusion.3
  95.5 0.1 broadcast_compare_fusion
  95.6 0.0 copy-done.5
  95.6 0.4 fusion.56
  96.0 1.2 fusion.17
  97.2 1.7 convolution_convert_fusion.3
  98.9 0.2 reshape_transpose_reshape.4
  99.1 5.4 %fusion.1 = bf16[4096,320]{0,1:T(8,128)(2,1)} fusion(bf16[320,512]{1,0:T(8,128)(2,1)S(1)} %reshape_transpose_reshape.4, bf16[512,4096]{1,0:T(8,128)(2,1)} %param.15), kind=kOutput, calls=%fused_computation.3 | convolution fusion | flops 1343488000 | bytes 7143424 | tf_op jit(solution)/shard_map/dot_general | solution.py:71
  104.5 0.0 reduce-scatter.2.cloned.1.call-update
  104.5 0.2 reshape_reshape_transpose_reshape.3
  104.7 1.3 fusion.9
  106.0 83.8 %all-to-all-done.1 = bf16[32,2,64,512]{3,2,1,0:T(8,128)(2,1)} async-done(((bf16[32,2,64,512]{3,2,1,0:T(8,128)(2,1)}), bf16[32,2,64,512]{3,2,1,0:T(8,128)(2,1)}, u32[]{:S(2)}, u32[]{:S(2)}) %all-to-all-start.1) | async-done | bytes 4194336 | tf_op jit(solution)/shard_map/all_to_all | solution.py:108
  189.7 6.7 %fusion.6 = bf16[20,64,512]{2,0,1:T(8,128)(2,1)S(1)} fusion(bf16[64,64,512]{2,1,0:T(8,128)(2,1)} %bitcast.14, s32[20]{0:T(128)S(1)} %multiply_add_fusion), kind=kOutput, calls=%fused_computation.10 | convolution fusion | flops 84542720 | bytes 5505104 | tf_op jit(solution)/shard_map/sr,skf->rkf/dot_general | solution.py:112
  196.5 0.5 fusion.20
  197.0 46.5 %psum.7 = bf16[20,16,64]{2,1,0:T(8,128)(2,1)S(1)} all-reduce(bf16[20,16,64]{2,1,0:T(8,128)(2,1)S(1)} %fusion.20), channel_id=1, replica_groups=mesh['rep'=32,'tp'=16] {'tp'}, use_global_device_ids=true, to_apply=%region_6.7 | all-reduce | flops 20480 | bytes 81920 | tf_op jit(solution)/shard_map/psum | solution.py:119
  243.5 0.2 fusion.19
  243.7 0.0 reduce-scatter.2.cloned.1.call-done
  243.7 1.6 fusion.30
  (7 shorter events, 0.0 us)
Async XLA Ops:
  6.5 88.2 %copy-start = (bf16[44,1,8,256]{3,2,1,0:T(8,128)(2,1)S(1)}, bf16[44,1,8,256]{3,2,1,0:T(8,128)(2,1)}, u32[]{:S(2)}) copy-start(bf16[44,1,8,256]{3,2,1,0:T(8,128)(2,1)} %param.12) | copy-start | bytes 540676
  34.2 4.2 %copy-start.2 = (bf16[2,64,512]{2,1,0:T(8,128)(2,1)S(1)}, bf16[2,64,512]{2,1,0:T(8,128)(2,1)}, u32[]{:S(2)}) copy-start(bf16[2,64,512]{2,1,0:T(8,128)(2,1)} %param.16) | copy-start | bytes 393220
  34.2 53.6 %all-to-all-start.2 = ((bf16[32,2,64,256]{3,2,1,0:T(8,128)(2,1)}), bf16[32,2,64,256]{3,2,1,0:T(8,128)(2,1)S(1)}, u32[]{:S(2)}, u32[]{:S(2)}) async-start(bf16[32,2,64,256]{3,2,1,0:T(8,128)(2,1)} %copy.44), calls=%async_computation.3 | async-start | bytes 4194304 | tf_op jit(solution)/shard_map/all_to_all | solution.py:109
  44.0 50.2 %copy-start.3 = (s32[20,6]{0,1:T(8,128)S(1)}, s32[20,6]{0,1:T(8,128)}, u32[]{:S(2)}) copy-start(s32[20,6]{0,1:T(8,128)} %param.14) | copy-start | bytes 1444
  44.0 50.5 %copy-start.1 = (bf16[320,512]{1,0:T(8,128)(2,1)S(1)}, bf16[320,512]{1,0:T(8,128)(2,1)}, u32[]{:S(2)}) copy-start(bf16[320,512]{1,0:T(8,128)(2,1)} %param.10) | copy-start | bytes 983044
  44.0 51.4 %copy-start.4 = (s32[20]{0:T(128)S(1)}, s32[20]{0:T(128)}, u32[]{:S(2)}) copy-start(s32[20]{0:T(128)} %param.13) | copy-start | bytes 244
  44.0 51.5 %copy-start.5 = (bf16[320,256]{1,0:T(8,128)(2,1)S(1)}, bf16[320,256]{1,0:T(8,128)(2,1)}, u32[]{:S(2)}) copy-start(bf16[320,256]{1,0:T(8,128)(2,1)} %param.11) | copy-start | bytes 491524
  87.8 101.9 %all-to-all-start.1 = ((bf16[32,2,64,512]{3,2,1,0:T(8,128)(2,1)}), bf16[32,2,64,512]{3,2,1,0:T(8,128)(2,1)}, u32[]{:S(2)}, u32[]{:S(2)}) async-start(bf16[32,2,64,512]{3,2,1,0:T(8,128)(2,1)} %copy.40), calls=%async_computation.2 | async-start | bytes 8388608 | tf_op jit(solution)/shard_map/all_to_all | solution.py:108
  94.0 149.7 %reduce-scatter.2.cloned.1.call-start = ((), (), s32[]{:S(2)}) async-start(), calls=%async_computation.4 | async-start | bytes 2785280 | tf_op jit(solution)/shard_map/reduce_scatter | solution.py:70
Sparse Core Ops, SparseCore 0:
  104.6 65.6 reduce-scatter.1
where the time goes:
time: 254 us; the launch traced here: 252 us
  waiting for transfers between devices  128 us (50%)
  blocking collectives  68.7 us (27%)
  matrix products  20.3 us (8%)
  between operations  13.6 us (5%)
  starting transfers between devices  10.6 us (4%)
  local copies, waits for them, and re-layouts  8.47 us (3%)
  other arithmetic  2.98 us (1%)
    all_to_all x1, waiting for transfers between devices, shards(): lax.all_to_all(down_blocks, 'rep', split_axis=0, concat_axis=0, tiled=True)  83.8 us
    psum x1, blocking collectives, shards(): down_projected = lax.psum(shrink_part.astype(jnp.bfloat16), 'tp')  46.5 us
    all_to_all x1, waiting for transfers between devices, shards(): lax.all_to_all(up_blocks, 'rep', split_axis=0, concat_axis=0, tiled=True)  43.8 us
    all_to_all x1, blocking collectives, shards(): lax.all_to_all(wanted, 'rep', split_axis=0, concat_axis=0, tiled=True)  22.2 us
    dot_general x1, matrix products, shards(): jnp.einsum('sr,skf->rkf', placing_mat, down_got, preferred_element_type=j...  6.75 us
    all_to_all x1, starting transfers between devices, shards(): lax.all_to_all(down_blocks, 'rep', split_axis=0, concat_axis=0, tiled=True)  6.2 us
    dot_general x1, matrix products, shards(): lax.dot_general(out_weight, attended, (((0,), (1,)), ((), ())), preferred...  5.37 us
  transfers between devices with their start and end apart: 3, of which 2 were waited for; matrix products, arithmetic and copies ran while one was open for 10% of the time, Pallas kernels for 0%

commit v1 on v0

--- a/solution.py
+++ b/solution.py
@@ -31,7 +31,6 @@
     heads_per_slot = head_count // slot_count
     cache_span = page_table.shape[1] * page_len
     output_columns = pooled_up_weight.shape[2]
-    rank_size = adapter_down.shape[1]
     paged_kv = (
         kv_cache[page_table]
         .transpose(0, 2, 1, 3, 4)
@@ -80,7 +79,6 @@
     )
     slot_hits = adapter_ids[:, None] == jnp.arange(pool_slot.shape[0])[None, :]
     pool_position = jnp.sum(jnp.where(slot_hits, pool_slot[None, :], 0), axis=1)
-    by_row = attended.reshape(row_count, per_row, feat_width)
     replicas = lax.axis_size("rep")
     local_count = adapter_down.shape[0]
     capacity = (row_count + replicas - 1) // replicas + 1
@@ -92,37 +90,41 @@
     target = owner_of * capacity + seat_of
     placing = jnp.arange(replicas * capacity)[:, None] == target[None, :]
     placing_mat = placing.astype(jnp.bfloat16)
-    wanted = (jnp.sum(jnp.where(placing, local_slot[None, :] + 1, 0), axis=1) - 1).reshape(
-        replicas, capacity
+    by_row = attended.reshape(row_count, per_row, feat_width)
+    send_rows = jnp.einsum(
+        "sr,rqf->sqf", placing_mat, by_row, preferred_element_type=jnp.float32
+    ).astype(jnp.bfloat16)
+    seat_slot = jnp.sum(jnp.where(placing, local_slot[None, :], 0), axis=1).astype(jnp.bfloat16)
+    marker = jnp.broadcast_to(seat_slot[:, None, None], (replicas * capacity, 1, feat_width))
+    payload = jnp.concatenate([send_rows, marker], axis=1).reshape(
+        replicas, capacity, per_row + 1, feat_width
     )
-    choose = (
-        lax.all_to_all(wanted, "rep", split_axis=0, concat_axis=0, tiled=True)[:, :, None]
-        == jnp.arange(local_count)[None, None, :]
-    ).astype(jnp.bfloat16)
-    down_blocks = jnp.einsum(
-        "smj,jkf->smkf", choose, adapter_down, preferred_element_type=jnp.float32
-    ).astype(jnp.bfloat16)
-    up_blocks = jnp.einsum(
-        "smj,jkd->smkd", choose, pooled_up_weight, preferred_element_type=jnp.float32
-    ).astype(jnp.bfloat16)
-    down_got = lax.all_to_all(down_blocks, "rep", split_axis=0, concat_axis=0, tiled=True)
-    up_got = lax.all_to_all(up_blocks, "rep", split_axis=0, concat_axis=0, tiled=True)
-    down_got = down_got.reshape(replicas * capacity, rank_size, feat_width)
-    up_got = up_got.reshape(replicas * capacity, rank_size, output_columns)
-    down_sel = jnp.einsum(
-        "sr,skf->rkf", placing_mat, down_got, preferred_element_type=jnp.float32
-    ).astype(jnp.bfloat16)
-    up_sel = jnp.einsum(
-        "sr,skd->rkd", placing_mat, up_got, preferred_element_type=jnp.float32
-    ).astype(jnp.bfloat16)
-    shrink_part = jnp.einsum("rqf,rkf->rqk", by_row, down_sel, preferred_element_type=jnp.float32)
+    arrived = lax.all_to_all(payload, "rep", split_axis=0, concat_axis=0, tiled=True)
+    arrived = arrived.reshape(replicas * capacity, per_row + 1, feat_width)
+    seat_rows = arrived[:, :per_row, :]
+    wants_one = arrived[:, per_row, 0] > 0.5
+    shrink_both = jnp.einsum(
+        "sqf,jkf->jsqk", seat_rows, adapter_down, preferred_element_type=jnp.float32
+    )
+    shrink_part = jnp.where(wants_one[:, None, None], shrink_both[1], shrink_both[0])
     down_projected = lax.psum(shrink_part.astype(jnp.bfloat16), "tp")
+    up_both = jnp.einsum(
+        "sqk,jkd->jsqd", down_projected, pooled_up_weight, preferred_element_type=jnp.float32
+    )
+    seat_delta = jnp.where(wants_one[:, None, None], up_both[1], up_both[0]).astype(jnp.bfloat16)
+    returned = lax.all_to_all(
+        seat_delta.reshape(replicas, capacity, per_row, output_columns),
+        "rep",
+        split_axis=0,
+        concat_axis=0,
+        tiled=True,
+    ).reshape(replicas * capacity, per_row, output_columns)
     adapter_correction = jnp.einsum(
-        "owe,oet->owt", down_projected, up_sel, preferred_element_type=jnp.float32
-    ).astype(jnp.bfloat16)
+        "sr,sqd->rqd", placing_mat, returned, preferred_element_type=jnp.float32
+    )
     adapted_output = plain_output + ADAPTER_SCALE * adapter_correction.reshape(
         token_count, output_columns
-    ).astype(jnp.float32)
+    )
     return adapted_output.astype(jnp.bfloat16)
 
 

time: 254 us -> 250 us (0.984)
  waiting for transfers between devices: 128 us -> 176 us
  blocking collectives: 68.7 us -> 24 us
  matrix products: 20.3 us -> 8.96 us
  starting transfers between devices: 10.6 us -> 13.8 us
  other arithmetic: 2.98 us -> 5.98 us
  local copies, waits for them, and re-layouts: 8.47 us -> 5.7 us
    psum x0 -> x1, waiting for transfers between devices: none -> 110 us  [shards(): down_projected = lax.psum(shrink_part.astype(jnp.bfloat16), 'tp')]
    all_to_all x2 -> x1, waiting for transfers between devices: 128 us -> 26.2 us  [shards(): lax.all_to_all(payload, 'rep', split_axis=0, concat_axis=0, tiled=True)]
    psum x1 -> x0, blocking collectives: 46.5 us -> none  [shards(): down_projected = lax.psum(shrink_part.astype(jnp.bfloat16), 'tp')]
    reduce_scatter x1, waiting for transfers between devices: 0.02 us -> 39.5 us  [shards(): lax.psum_scatter(lax.dot_general(out_weight, attended, (((0,), (1,)), (()...]
    dot_general x6 -> x4, matrix products: 11.6 us -> 2.65 us  [the longest x1 1.36 us: shards(): jnp.einsum('sqk,jkd->jsqd', down_projected, pooled_up_weight, preferred_e...]
    convert_element_type x2 -> x0, local copies, waits for them, and re-layouts: 6.82 us -> none  [the longest x1 4.3 us: shards(): down_blocks = jnp.einsum('smj,jkf->smkf', choose, adapter_down, preferred...]
    all_to_all x2 -> x1, starting transfers between devices: 10.3 us -> 13.7 us  [shards(): lax.all_to_all(payload, 'rep', split_axis=0, concat_axis=0, tiled=True)]
  transfers between devices with their start and end apart: 3 -> 3, of which waited for: 2 -> 3; matrix products, arithmetic and copies ran while one was open for 10% -> 3% of each run, Pallas kernels for 0% -> 0%
where the time goes in v1:
time: 250 us; the launch traced here: 248 us
  waiting for transfers between devices  176 us (70%)
  blocking collectives  24 us (10%)
  starting transfers between devices  13.8 us (6%)
  between operations  13.6 us (5%)
  matrix products  8.96 us (4%)
  other arithmetic  5.98 us (2%)
  local copies, waits for them, and re-layouts  5.7 us (2%)
    psum x1, waiting for transfers between devices, shards(): down_projected = lax.psum(shrink_part.astype(jnp.bfloat16), 'tp')  110 us
    reduce_scatter x1, waiting for transfers between devices, shards(): lax.psum_scatter(lax.dot_general(out_weight, attended, (((0,), (1,)), (()...  39.5 us
    all_to_all x1, waiting for transfers between devices, shards(): lax.all_to_all(payload, 'rep', split_axis=0, concat_axis=0, tiled=True)  26.2 us
    all_to_all x1, blocking collectives, shards(): lax.all_to_all(seat_delta.reshape(replicas, capacity, per_row, output_col...  24 us
    all_to_all x1, starting transfers between devices, shards(): lax.all_to_all(payload, 'rep', split_axis=0, concat_axis=0, tiled=True)  13.7 us
    dot_general x1, matrix products, shards(): lax.dot_general(out_weight, attended, (((0,), (1,)), ((), ())), preferred...  5.22 us
  transfers between devices with their start and end apart: 3, of which 3 were waited for; matrix products, arithmetic and copies ran while one was open for 3% of the time, Pallas kernels for 0%

profile of v1, /device:TPU:1, one launch (start us, length us, event | category | flops | bytes accessed | tf_op | source)
XLA Modules:
  0.0 248.2 jit_solution(3435918056866313754)
XLA Ops:
  6.5 0.0 copy-start
  6.5 0.8 iota_compare_fusion.3
  7.3 0.7 compare_select_fusion
  8.0 0.1 copy.33
  8.1 0.1 reshape.203
  8.2 1.2 reshape.194
  9.4 0.1 broadcast_compare_fusion
  9.5 0.0 copy-done
  9.5 0.7 gather_fusion
  10.2 0.4 fusion.37
  10.6 0.0 copy-start.4
  10.6 0.0 copy-start.5
  10.6 0.3 fusion.5
  10.9 0.3 copy-done.4
  11.3 0.0 copy-done.5
  11.3 0.2 select_reduce_fusion.1
  11.5 0.2 convert_reduce_fusion
  11.7 0.1 select_reduce_fusion
  11.8 0.3 convolution_convert_fusion.2
  12.1 0.2 reshape_reshape_transpose_reshape.3
  12.3 0.6 convolution_convert_fusion.1
  12.9 0.1 broadcast_in_dim.107
  13.0 0.1 pad_maximum_fusion
  13.1 0.5 reshape.196
  13.5 1.8 copy.36
  15.3 13.7 %all-to-all-start = ((bf16[32,2,17,512]{3,1,2,0:T(2,128)(2,1)}), bf16[32,2,17,512]{3,1,2,0:T(2,128)(2,1)S(1)}, u32[]{:S(2)}, u32[]{:S(2)}) async-start(bf16[32,2,17,512]{3,1,2,0:T(2,128)(2,1)} %copy.36), calls=%async_computation.1 | async-start | bytes 2228224 | tf_op jit(solution)/shard_map/all_to_all | solution.py:102
  29.0 0.0 copy-start.3
  29.0 0.0 all-reduce.2.cloned.1.call-start
  29.1 0.2 reshape_transpose_reshape.4
  29.3 26.2 %all-to-all-done = bf16[32,2,17,512]{3,1,2,0:T(2,128)(2,1)S(1)} async-done(((bf16[32,2,17,512]{3,1,2,0:T(2,128)(2,1)}), bf16[32,2,17,512]{3,1,2,0:T(2,128)(2,1)S(1)}, u32[]{:S(2)}, u32[]{:S(2)}) %all-to-all-start) | async-done | bytes 1114144 | tf_op jit(solution)/shard_map/all_to_all | solution.py:102
  55.5 0.3 copy.37
  55.8 1.2 compare_reduce_fusion
  57.1 0.5 convolution_bitcast_fusion.1
  57.5 0.9 fusion.7
  58.4 0.0 all-reduce.2.cloned.1.call-update
  58.4 0.0 reduce-scatter.2.cloned.1.call-start
  58.4 5.2 %fusion.1 = bf16[4096,320]{0,1:T(8,128)(2,1)} fusion(bf16[320,512]{1,0:T(8,128)(2,1)S(1)} %reshape_transpose_reshape.4, bf16[512,4096]{1,0:T(8,128)(2,1)} %param.15), kind=kOutput, calls=%fused_computation.3 | convolution fusion | flops 1343488000 | bytes 7143424 | tf_op jit(solution)/shard_map/dot_general | solution.py:70
  63.7 0.0 reduce-scatter.2.cloned.1.call-update
  63.7 0.1 broadcast_in_dim.108
  63.8 110.3 %all-reduce.2.cloned.1.call-done = bf16[64,16,64]{2,1,0:T(8,128)(2,1)} async-done(((bf16[64,16,64]{2,1,0:T(8,128)(2,1)}), bf16[64,16,64]{2,1,0:T(8,128)(2,1)}) %all-reduce.2.cloned.1.call-update) | async-done | bytes 131088 | tf_op jit(solution)/shard_map/psum | solution.py:110
  174.1 1.4 convolution_bitcast_fusion
  175.5 0.1 fusion.36
  175.6 0.1 select_convert_fusion
  175.7 24.0 %all_to_all.10 = bf16[32,2,16,256]{3,2,1,0:T(8,128)(2,1)S(1)} all-to-all(bf16[32,2,16,256]{3,2,1,0:T(8,128)(2,1)S(1)} %select_convert_fusion), channel_id=1, replica_groups=mesh['rep'=32,'tp'=16] {'rep'}, dimensions={0} | all-to-all | bytes 1048576 | tf_op jit(solution)/shard_map/all_to_all | solution.py:115
  199.8 0.3 convolution_multiply_fusion.1
  200.1 0.1 copy.40
  200.2 39.5 %reduce-scatter.2.cloned.1.call-done = bf16[256,320]{0,1:T(8,128)(2,1)} async-done(((bf16[4096,320]{0,1:T(8,128)(2,1)}), bf16[256,320]{0,1:T(8,128)(2,1)}) %reduce-scatter.2.cloned.1.call-update) | async-done | bytes 163856 | tf_op jit(solution)/shard_map/reduce_scatter | solution.py:69
  239.7 1.6 fusion.16
  (11 shorter events, 0.1 us)
Async XLA Ops:
  6.5 2.9 %copy-start = (bf16[44,1,8,256]{3,2,1,0:T(8,128)(2,1)S(1)}, bf16[44,1,8,256]{3,2,1,0:T(8,128)(2,1)}, u32[]{:S(2)}) copy-start(bf16[44,1,8,256]{3,2,1,0:T(8,128)(2,1)} %param.12) | copy-start | bytes 540676
  6.5 3.6 %copy-start.2 = (bf16[320,256]{1,0:T(8,128)(2,1)S(1)}, bf16[320,256]{1,0:T(8,128)(2,1)}, u32[]{:S(2)}) copy-start(bf16[320,256]{1,0:T(8,128)(2,1)} %param.11) | copy-start | bytes 491524
  10.6 0.7 copy-start.4
  10.6 0.7 copy-start.5
  15.3 40.2 %all-to-all-start = ((bf16[32,2,17,512]{3,1,2,0:T(2,128)(2,1)}), bf16[32,2,17,512]{3,1,2,0:T(2,128)(2,1)S(1)}, u32[]{:S(2)}, u32[]{:S(2)}) async-start(bf16[32,2,17,512]{3,1,2,0:T(2,128)(2,1)} %copy.36), calls=%async_computation.1 | async-start | bytes 2228224 | tf_op jit(solution)/shard_map/all_to_all | solution.py:102
  29.0 28.0 %copy-start.3 = (bf16[2,64,512]{2,1,0:T(8,128)(2,1)S(1)}, bf16[2,64,512]{2,1,0:T(8,128)(2,1)}, u32[]{:S(2)}) copy-start(bf16[2,64,512]{2,1,0:T(8,128)(2,1)} %param.16) | copy-start | bytes 393220
  29.0 145.1 %all-reduce.2.cloned.1.call-start = ((), (), s32[]{:S(2)}) async-start(), calls=%async_computation.4 | async-start | bytes 524288 | tf_op jit(solution)/shard_map/psum | solution.py:110
  58.4 181.3 %reduce-scatter.2.cloned.1.call-start = ((), (), s32[]{:S(2)}) async-start(), calls=%async_computation.3 | async-start | bytes 2785280 | tf_op jit(solution)/shard_map/reduce_scatter | solution.py:69
  63.7 110.5 %copy-start.1 = (bf16[2,64,256]{2,1,0:T(8,128)(2,1)S(1)}, bf16[2,64,256]{2,1,0:T(8,128)(2,1)}, u32[]{:S(2)}) copy-start(bf16[2,64,256]{2,1,0:T(8,128)(2,1)} %param.17) | copy-start | bytes 196612
Sparse Core Ops, SparseCore 0:
  58.5 115.5 all-reduce.1
  177.0 62.6 reduce-scatter.1

commit v2 on v1

--- a/solution.py
+++ b/solution.py
@@ -6,6 +6,17 @@
 from jax.sharding import PartitionSpec as P
 
 ADAPTER_SCALE = 2.0
+
+
+def tp_sum(part):
+    width = lax.axis_size("tp")
+    chunks = part.reshape(width, -1)
+    gathered = lax.all_to_all(chunks, "tp", split_axis=0, concat_axis=0, tiled=True)
+    summed = jnp.sum(gathered.astype(jnp.float32), axis=0, keepdims=True).astype(jnp.bfloat16)
+    spread = lax.all_to_all(
+        jnp.broadcast_to(summed, chunks.shape), "tp", split_axis=0, concat_axis=0, tiled=True
+    )
+    return spread.reshape(part.shape)
 
 
 def shards(
@@ -107,7 +118,7 @@
         "sqf,jkf->jsqk", seat_rows, adapter_down, preferred_element_type=jnp.float32
     )
     shrink_part = jnp.where(wants_one[:, None, None], shrink_both[1], shrink_both[0])
-    down_projected = lax.psum(shrink_part.astype(jnp.bfloat16), "tp")
+    down_projected = tp_sum(shrink_part.astype(jnp.bfloat16))
     up_both = jnp.einsum(
         "sqk,jkd->jsqd", down_projected, pooled_up_weight, preferred_element_type=jnp.float32
     )

time: 250 us -> 129 us (0.52)
  the two profiles are of different devices: /device:TPU:1 before, /device:TPU:64 now
where the time goes in v2:
time: 129 us; the launch traced here: 128 us
  blocking collectives  39.3 us (30%)
  waiting for transfers between devices  33.8 us (26%)
  starting transfers between devices  16.1 us (12%)
  between operations  13.7 us (11%)
  local copies, waits for them, and re-layouts  8.7 us (7%)
  other arithmetic  8.35 us (6%)
  matrix products  8.09 us (6%)
    all_to_all x1, waiting for transfers between devices, shards(): lax.all_to_all(payload, 'rep', split_axis=0, concat_axis=0, tiled=True)  24.3 us
    all_to_all x1, blocking collectives, shards(): lax.all_to_all(seat_delta.reshape(replicas, capacity, per_row, output_col...  23 us
    all_to_all x1, blocking collectives, tp_sum(): lax.all_to_all(chunks, 'tp', split_axis=0, concat_axis=0, tiled=True)  16.3 us
    all_to_all x1, starting transfers between devices, shards(): lax.all_to_all(payload, 'rep', split_axis=0, concat_axis=0, tiled=True)  12.6 us
    all_to_all x1, waiting for transfers between devices, tp_sum(): lax.all_to_all(jnp.broadcast_to(summed, chunks.shape), 'tp', split_axis=0...  9.49 us
    dot_general x1, matrix products, shards(): lax.dot_general(out_weight, attended, (((0,), (1,)), ((), ())), preferred...  5.31 us
    all_to_all x1, starting transfers between devices, tp_sum(): lax.all_to_all(jnp.broadcast_to(summed, chunks.shape), 'tp', split_axis=0...  3.51 us
  transfers between devices with their start and end apart: 3, of which 2 were waited for; matrix products, arithmetic and copies ran while one was open for 12% of the time, Pallas kernels for 0%

profile of v2, /device:TPU:64, one launch (start us, length us, event | category | flops | bytes accessed | tf_op | source)
XLA Modules:
  0.0 128.1 jit_solution(13875519412085633874)
XLA Ops:
  6.5 0.8 iota_compare_fusion.3
  7.3 0.7 compare_select_fusion
  8.0 0.1 copy.40
  8.2 1.2 reshape.241
  9.5 0.7 gather_fusion
  10.2 0.4 fusion.36
  10.6 0.3 fusion.5
  10.9 0.3 copy-done.4
  11.3 0.2 select_reduce_fusion.1
  11.5 0.2 convert_reduce_fusion
  11.7 0.1 select_reduce_fusion
  11.8 0.3 convolution_convert_fusion.2
  12.1 0.2 reshape_reshape_transpose_reshape.3
  12.3 0.6 convolution_convert_fusion.1
  13.0 0.1 pad_maximum_fusion
  13.1 0.5 reshape.243
  13.5 1.8 %copy.43 = bf16[32,2,17,512]{3,1,2,0:T(2,128)(2,1)} copy(bf16[32,2,17,512]{3,1,0,2:T(2,128)(2,1)S(1)} %reshape.243) | data formatting | bytes 2228224 | tf_op jit(solution)/shard_map/reshape | solution.py:110
  15.3 12.6 %all-to-all-start = ((bf16[32,2,17,512]{3,1,2,0:T(2,128)(2,1)}), bf16[32,2,17,512]{3,1,2,0:T(2,128)(2,1)S(1)}, u32[]{:S(2)}, u32[]{:S(2)}) async-start(bf16[32,2,17,512]{3,1,2,0:T(2,128)(2,1)} %copy.43), calls=%async_computation.1 | async-start | bytes 2228224 | tf_op jit(solution)/shard_map/all_to_all | solution.py:113
  28.0 0.2 reshape_transpose_reshape.4
  28.2 5.3 %fusion.1 = bf16[4096,320]{0,1:T(8,128)(2,1)} fusion(bf16[320,512]{1,0:T(8,128)(2,1)S(1)} %reshape_transpose_reshape.4, bf16[512,4096]{1,0:T(8,128)(2,1)} %param.15), kind=kOutput, calls=%fused_computation.3 | convolution fusion | flops 1343488000 | bytes 7143424 | tf_op jit(solution)/shard_map/dot_general | solution.py:81
  33.5 24.3 %all-to-all-done = bf16[32,2,17,512]{3,1,2,0:T(2,128)(2,1)S(1)} async-done(((bf16[32,2,17,512]{3,1,2,0:T(2,128)(2,1)}), bf16[32,2,17,512]{3,1,2,0:T(2,128)(2,1)S(1)}, u32[]{:S(2)}, u32[]{:S(2)}) %all-to-all-start) | async-done | bytes 1114144 | tf_op jit(solution)/shard_map/all_to_all | solution.py:113
  57.8 0.3 copy.44
  58.1 0.4 convolution_bitcast_fusion.1
  58.6 0.3 squeeze.14
  58.9 1.2 compare_reduce_fusion
  60.1 0.1 broadcast_in_dim.119
  60.3 0.2 broadcast_in_dim.120
  60.5 0.3 squeeze.13
  60.9 0.5 broadcast.242
  61.4 0.7 reduce.10
  62.1 16.3 %all_to_all.22 = bf16[16,2,2048]{2,1,0:T(2,128)(2,1)S(1)} all-to-all(bf16[16,2,2048]{2,1,0:T(2,128)(2,1)S(1)} %reshape.270), channel_id=1, replica_groups=mesh['rep'=32,'tp'=16] {'tp'}, dimensions={0} | all-to-all | bytes 262144 | tf_op jit(solution)/shard_map/all_to_all | solution.py:14
  78.5 0.1 reshape.271
  78.6 0.2 reduce_sum.52
  78.8 0.2 broadcast_in_dim.121
  79.0 1.4 %reduce.11 = bf16[16,4096]{1,0:T(8,128)(2,1)S(1)} reduce(bf16[16,1,4096]{2,1,0:T(2,128)(2,1)S(1)} %broadcast_in_dim.121, bf16[]{:T(256)} %broadcast.242), dimensions={1}, to_apply=%broadcast_in_dim.121.reduce_sub_computation | reduce | bytes 262146 | tf_op jit(solution)/shard_map/broadcast_in_dim | solution.py:17
  80.5 0.7 reshape.272
  81.2 3.5 %all-to-all-start.2 = ((bf16[16,2,2048]{2,1,0:T(2,128)(2,1)}), bf16[16,2,2048]{2,1,0:T(2,128)(2,1)S(1)}, u32[]{:S(2)}, u32[]{:S(2)}) async-start(bf16[16,2,2048]{2,1,0:T(2,128)(2,1)} %reshape.272), calls=%async_computation.3 | async-start | bytes 262144 | tf_op jit(solution)/shard_map/all_to_all | solution.py:16
  84.7 0.1 broadcast_in_dim.116
  84.9 9.5 %all-to-all-done.2 = bf16[16,2,2048]{2,1,0:T(2,128)(2,1)S(1)} async-done(((bf16[16,2,2048]{2,1,0:T(2,128)(2,1)}), bf16[16,2,2048]{2,1,0:T(2,128)(2,1)S(1)}, u32[]{:S(2)}, u32[]{:S(2)}) %all-to-all-start.2) | async-done | bytes 131104 | tf_op jit(solution)/shard_map/all_to_all | solution.py:16
  94.3 0.1 reshape.273
  94.5 0.8 reduce.8
  95.3 0.2 reshape.264
  95.5 0.4 convolution_bitcast_fusion
  96.0 0.1 select_convert_fusion
  96.2 23.0 %all_to_all.23 = bf16[32,2,16,256]{3,2,1,0:T(8,128)(2,1)S(1)} all-to-all(bf16[32,2,16,256]{3,2,1,0:T(8,128)(2,1)S(1)} %select_convert_fusion), channel_id=1, replica_groups=mesh['rep'=32,'tp'=16] {'rep'}, dimensions={0} | all-to-all | bytes 1048576 | tf_op jit(solution)/shard_map/all_to_all | solution.py:126
  119.2 0.3 convolution_multiply_fusion.1
  119.5 0.1 copy.47
  119.6 1.6 %fusion.14 = bf16[320,256]{1,0:T(8,128)(2,1)} fusion(f32[20,16,256]{2,1,0:T(8,128)S(1)} %copy.47, bf16[256,320]{0,1:T(8,128)(2,1)} %reduce-scatter.2.cloned.1.call-done), kind=kLoop, calls=%fused_computation.28 | loop fusion | flops 245760 | bytes 655360 | tf_op jit(solution)/shard_map/convert_element_type | solution.py:139
  (27 shorter events, 0.6 us)
Async XLA Ops:
  6.5 2.9 %copy-start = (bf16[44,1,8,256]{3,2,1,0:T(8,128)(2,1)S(1)}, bf16[44,1,8,256]{3,2,1,0:T(8,128)(2,1)}, u32[]{:S(2)}) copy-start(bf16[44,1,8,256]{3,2,1,0:T(8,128)(2,1)} %param.12) | copy-start | bytes 540676
  6.5 3.6 %copy-start.2 = (bf16[320,256]{1,0:T(8,128)(2,1)S(1)}, bf16[320,256]{1,0:T(8,128)(2,1)}, u32[]{:S(2)}) copy-start(bf16[320,256]{1,0:T(8,128)(2,1)} %param.11) | copy-start | bytes 491524
  10.6 0.7 copy-start.4
  10.6 0.7 copy-start.5
  15.3 42.5 %all-to-all-start = ((bf16[32,2,17,512]{3,1,2,0:T(2,128)(2,1)}), bf16[32,2,17,512]{3,1,2,0:T(2,128)(2,1)S(1)}, u32[]{:S(2)}, u32[]{:S(2)}) async-start(bf16[32,2,17,512]{3,1,2,0:T(2,128)(2,1)} %copy.43), calls=%async_computation.1 | async-start | bytes 2228224 | tf_op jit(solution)/shard_map/all_to_all | solution.py:113
  27.9 91.7 %reduce-scatter.2.cloned.1.call-start = ((), (), s32[]{:S(2)}) async-start(), calls=%async_computation.5 | async-start | bytes 2785280 | tf_op jit(solution)/shard_map/reduce_scatter | solution.py:80
  33.5 24.6 %copy-start.3 = (bf16[2,64,512]{2,1,0:T(8,128)(2,1)S(1)}, bf16[2,64,512]{2,1,0:T(8,128)(2,1)}, u32[]{:S(2)}) copy-start(bf16[2,64,512]{2,1,0:T(8,128)(2,1)} %param.16) | copy-start | bytes 393220
  78.5 17.1 %copy-start.1 = (bf16[2,64,256]{2,1,0:T(8,128)(2,1)S(1)}, bf16[2,64,256]{2,1,0:T(8,128)(2,1)}, u32[]{:S(2)}) copy-start(bf16[2,64,256]{2,1,0:T(8,128)(2,1)} %param.17) | copy-start | bytes 196612
  81.2 13.1 %all-to-all-start.2 = ((bf16[16,2,2048]{2,1,0:T(2,128)(2,1)}), bf16[16,2,2048]{2,1,0:T(2,128)(2,1)S(1)}, u32[]{:S(2)}, u32[]{:S(2)}) async-start(bf16[16,2,2048]{2,1,0:T(2,128)(2,1)} %reshape.272), calls=%async_computation.3 | async-start | bytes 262144 | tf_op jit(solution)/shard_map/all_to_all | solution.py:16
Sparse Core Ops, SparseCore 0:
  33.6 67.3 reduce-scatter.1

commit v3 on v2

--- a/solution.py
+++ b/solution.py
@@ -76,18 +76,12 @@
         0, 2, 1, 3, 4
     )
     attended = attended.reshape(token_count, feat_width)
-    plain_output = (
-        lax.psum_scatter(
-            lax.dot_general(
-                out_weight, attended, (((0,), (1,)), ((), ())), preferred_element_type=jnp.float32
-            ).astype(jnp.bfloat16),
-            "tp",
-            scatter_dimension=0,
-            tiled=True,
-        )
-        .astype(jnp.float32)
-        .T
-    )
+    plain_output = lax.psum_scatter(
+        jnp.dot(attended, out_weight, preferred_element_type=jnp.float32).astype(jnp.bfloat16),
+        "tp",
+        scatter_dimension=1,
+        tiled=True,
+    ).astype(jnp.float32)
     slot_hits = adapter_ids[:, None] == jnp.arange(pool_slot.shape[0])[None, :]
     pool_position = jnp.sum(jnp.where(slot_hits, pool_slot[None, :], 0), axis=1)
     replicas = lax.axis_size("rep")
@@ -113,16 +107,18 @@
     arrived = lax.all_to_all(payload, "rep", split_axis=0, concat_axis=0, tiled=True)
     arrived = arrived.reshape(replicas * capacity, per_row + 1, feat_width)
     seat_rows = arrived[:, :per_row, :]
-    wants_one = arrived[:, per_row, 0] > 0.5
+    rank_size = adapter_down.shape[1]
+    wants_one = arrived[:, per_row, :rank_size] > 0.5
+    wants_one_out = arrived[:, per_row, :output_columns] > 0.5
     shrink_both = jnp.einsum(
         "sqf,jkf->jsqk", seat_rows, adapter_down, preferred_element_type=jnp.float32
     )
-    shrink_part = jnp.where(wants_one[:, None, None], shrink_both[1], shrink_both[0])
+    shrink_part = jnp.where(wants_one[:, None, :], shrink_both[1], shrink_both[0])
     down_projected = tp_sum(shrink_part.astype(jnp.bfloat16))
     up_both = jnp.einsum(
         "sqk,jkd->jsqd", down_projected, pooled_up_weight, preferred_element_type=jnp.float32
     )
-    seat_delta = jnp.where(wants_one[:, None, None], up_both[1], up_both[0]).astype(jnp.bfloat16)
+    seat_delta = jnp.where(wants_one_out[:, None, :], up_both[1], up_both[0]).astype(jnp.bfloat16)
     returned = lax.all_to_all(
         seat_delta.reshape(replicas, capacity, per_row, output_columns),
         "rep",

time: 129 us -> 127 us (0.984)
  the two profiles are of different devices: /device:TPU:64 before, /device:TPU:1 now
where the time goes in v3:
time: 127 us
  blocking collectives  41.4 us (33%)
  waiting for transfers between devices  30.5 us (24%)
  starting transfers between devices  17.3 us (14%)
  between operations  13.7 us (11%)
  local copies, waits for them, and re-layouts  8.53 us (7%)
  matrix products  8.07 us (6%)
  other arithmetic  7.26 us (6%)
    all_to_all x1, blocking collectives, tp_sum(): lax.all_to_all(chunks, 'tp', split_axis=0, concat_axis=0, tiled=True)  21.2 us
    all_to_all x1, waiting for transfers between devices, shards(): lax.all_to_all(payload, 'rep', split_axis=0, concat_axis=0, tiled=True)  20.9 us
    all_to_all x1, blocking collectives, shards(): lax.all_to_all(seat_delta.reshape(replicas, capacity, per_row, output_col...  20.1 us
    all_to_all x1, starting transfers between devices, shards(): lax.all_to_all(payload, 'rep', split_axis=0, concat_axis=0, tiled=True)  13.7 us
    all_to_all x1, waiting for transfers between devices, tp_sum(): lax.all_to_all(jnp.broadcast_to(summed, chunks.shape), 'tp', split_axis=0...  9.56 us
    dot_general x1, matrix products, shards(): jnp.dot(attended, out_weight, preferred_element_type=jnp.float32)  5.3 us
    all_to_all x1, starting transfers between devices, tp_sum(): lax.all_to_all(jnp.broadcast_to(summed, chunks.shape), 'tp', split_axis=0...  3.52 us
  transfers between devices with their start and end apart: 3, of which 2 were waited for; matrix products, arithmetic and copies ran while one was open for 11% of the time, Pallas kernels for 0%

profile of v3, /device:TPU:1, one launch (start us, length us, event | category | flops | bytes accessed | tf_op | source)
XLA Modules:
  0.0 126.7 jit_solution(2026725912752047001)
XLA Ops:
  6.5 0.8 iota_compare_fusion.3
  7.3 0.7 compare_select_fusion
  8.0 0.1 copy.40
  8.1 0.1 reshape.251
  8.2 1.2 reshape.241
  9.5 0.7 gather_fusion
  10.2 0.4 fusion.35
  10.6 0.3 fusion.4
  10.9 0.3 copy-done.4
  11.3 0.2 select_reduce_fusion.1
  11.5 0.2 convert_reduce_fusion
  11.7 0.1 select_reduce_fusion
  11.8 0.3 convolution_convert_fusion.2
  12.1 0.2 reshape_reshape_transpose_reshape.3
  12.3 0.6 convolution_convert_fusion.1
  13.0 0.1 pad_maximum_fusion
  13.1 0.5 reshape.243
  13.5 1.8 %copy.43 = bf16[32,2,17,512]{3,1,2,0:T(2,128)(2,1)} copy(bf16[32,2,17,512]{3,1,0,2:T(2,128)(2,1)S(1)} %reshape.243) | data formatting | bytes 2228224 | tf_op jit(solution)/shard_map/reshape | solution.py:104
  15.3 13.7 %all-to-all-start = ((bf16[32,2,17,512]{3,1,2,0:T(2,128)(2,1)}), bf16[32,2,17,512]{3,1,2,0:T(2,128)(2,1)S(1)}, u32[]{:S(2)}, u32[]{:S(2)}) async-start(bf16[32,2,17,512]{3,1,2,0:T(2,128)(2,1)} %copy.43), calls=%async_computation.1 | async-start | bytes 2228224 | tf_op jit(solution)/shard_map/all_to_all | solution.py:107
  29.1 0.2 reshape_transpose_reshape.4
  29.3 5.3 %convolution_convert_fusion = bf16[320,4096]{1,0:T(8,128)(2,1)} fusion(bf16[320,512]{1,0:T(8,128)(2,1)S(1)} %reshape_transpose_reshape.4, bf16[512,4096]{1,0:T(8,128)(2,1)} %param.15), kind=kOutput, calls=%fused_computation.2 | convolution fusion | flops 1343488000 | bytes 7143424 | tf_op jit(solution)/shard_map/dot_general | solution.py:80
  34.6 20.9 %all-to-all-done = bf16[32,2,17,512]{3,1,2,0:T(2,128)(2,1)S(1)} async-done(((bf16[32,2,17,512]{3,1,2,0:T(2,128)(2,1)}), bf16[32,2,17,512]{3,1,2,0:T(2,128)(2,1)S(1)}, u32[]{:S(2)}, u32[]{:S(2)}) %all-to-all-start) | async-done | bytes 1114144 | tf_op jit(solution)/shard_map/all_to_all | solution.py:107
  55.5 0.3 copy.44
  55.9 0.4 convolution_bitcast_fusion.1
  56.4 0.3 squeeze.15
  56.7 0.2 broadcast_in_dim.120
  57.0 0.3 squeeze.14
  57.3 0.5 broadcast.242
  57.8 0.7 reduce.9
  58.5 0.1 reshape.269
  58.6 21.2 %all_to_all.22 = bf16[16,2,2048]{2,1,0:T(2,128)(2,1)S(1)} all-to-all(bf16[16,2,2048]{2,1,0:T(2,128)(2,1)S(1)} %reshape.269), channel_id=1, replica_groups=mesh['rep'=32,'tp'=16] {'tp'}, dimensions={0} | all-to-all | bytes 262144 | tf_op jit(solution)/shard_map/all_to_all | solution.py:14
  79.8 0.1 reshape.270
  79.9 0.2 reduce_sum.52
  80.2 0.2 broadcast_in_dim.121
  80.4 1.4 %reduce.10 = bf16[16,4096]{1,0:T(8,128)(2,1)S(1)} reduce(bf16[16,1,4096]{2,1,0:T(2,128)(2,1)S(1)} %broadcast_in_dim.121, bf16[]{:T(256)} %broadcast.242), dimensions={1}, to_apply=%broadcast_in_dim.121.reduce_sub_computation | reduce | bytes 262146 | tf_op jit(solution)/shard_map/broadcast_in_dim | solution.py:17
  81.8 0.7 reshape.271
  82.5 3.5 %all-to-all-start.2 = ((bf16[16,2,2048]{2,1,0:T(2,128)(2,1)}), bf16[16,2,2048]{2,1,0:T(2,128)(2,1)S(1)}, u32[]{:S(2)}, u32[]{:S(2)}) async-start(bf16[16,2,2048]{2,1,0:T(2,128)(2,1)} %reshape.271), calls=%async_computation.3 | async-start | bytes 262144 | tf_op jit(solution)/shard_map/all_to_all | solution.py:16
  86.1 0.2 compare_reduce_fusion
  86.3 9.6 %all-to-all-done.2 = bf16[16,2,2048]{2,1,0:T(2,128)(2,1)S(1)} async-done(((bf16[16,2,2048]{2,1,0:T(2,128)(2,1)}), bf16[16,2,2048]{2,1,0:T(2,128)(2,1)S(1)}, u32[]{:S(2)}, u32[]{:S(2)}) %all-to-all-start.2) | async-done | bytes 131104 | tf_op jit(solution)/shard_map/all_to_all | solution.py:16
  95.9 0.1 reshape.272
  96.0 0.8 reduce.7
  96.8 0.2 reshape.264
  97.0 0.4 convolution_bitcast_fusion
  97.5 0.1 select_convert_fusion
  97.6 20.1 %all_to_all.23 = bf16[32,2,16,256]{3,2,1,0:T(8,128)(2,1)S(1)} all-to-all(bf16[32,2,16,256]{3,2,1,0:T(8,128)(2,1)S(1)} %select_convert_fusion), channel_id=1, replica_groups=mesh['rep'=32,'tp'=16] {'rep'}, dimensions={0} | all-to-all | bytes 1048576 | tf_op jit(solution)/shard_map/all_to_all | solution.py:122
  117.8 0.3 convolution_multiply_fusion.1
  118.0 0.1 copy.47
  118.2 1.6 %fusion.13 = bf16[320,256]{1,0:T(8,128)(2,1)} fusion(f32[20,16,256]{2,1,0:T(8,128)S(1)} %copy.47, bf16[320,256]{1,0:T(8,128)(2,1)} %reduce-scatter.2.cloned.1.call-done), kind=kLoop, calls=%fused_computation.27 | loop fusion | flops 245760 | bytes 655360 | tf_op jit(solution)/shard_map/convert_element_type | solution.py:135
  (29 shorter events, 0.6 us)
Async XLA Ops:
  6.5 2.9 %copy-start = (bf16[44,1,8,256]{3,2,1,0:T(8,128)(2,1)S(1)}, bf16[44,1,8,256]{3,2,1,0:T(8,128)(2,1)}, u32[]{:S(2)}) copy-start(bf16[44,1,8,256]{3,2,1,0:T(8,128)(2,1)} %param.12) | copy-start | bytes 540676
  6.5 3.6 %copy-start.2 = (bf16[320,256]{1,0:T(8,128)(2,1)S(1)}, bf16[320,256]{1,0:T(8,128)(2,1)}, u32[]{:S(2)}) copy-start(bf16[320,256]{1,0:T(8,128)(2,1)} %param.11) | copy-start | bytes 491524
  10.6 0.7 copy-start.4
  10.6 0.7 copy-start.5
  15.3 40.2 %all-to-all-start = ((bf16[32,2,17,512]{3,1,2,0:T(2,128)(2,1)}), bf16[32,2,17,512]{3,1,2,0:T(2,128)(2,1)S(1)}, u32[]{:S(2)}, u32[]{:S(2)}) async-start(bf16[32,2,17,512]{3,1,2,0:T(2,128)(2,1)} %copy.43), calls=%async_computation.1 | async-start | bytes 2228224 | tf_op jit(solution)/shard_map/all_to_all | solution.py:107
  29.0 89.1 %reduce-scatter.2.cloned.1.call-start = ((), (), s32[]{:S(2)}) async-start(), calls=%async_computation.5 | async-start | bytes 2785280 | tf_op jit(solution)/shard_map/reduce_scatter | solution.py:79
  34.6 21.3 %copy-start.3 = (bf16[2,64,512]{2,1,0:T(8,128)(2,1)S(1)}, bf16[2,64,512]{2,1,0:T(8,128)(2,1)}, u32[]{:S(2)}) copy-start(bf16[2,64,512]{2,1,0:T(8,128)(2,1)} %param.16) | copy-start | bytes 393220
  79.8 17.2 %copy-start.1 = (bf16[2,64,256]{2,1,0:T(8,128)(2,1)S(1)}, bf16[2,64,256]{2,1,0:T(8,128)(2,1)}, u32[]{:S(2)}) copy-start(bf16[2,64,256]{2,1,0:T(8,128)(2,1)} %param.17) | copy-start | bytes 196612
  82.5 13.3 %all-to-all-start.2 = ((bf16[16,2,2048]{2,1,0:T(2,128)(2,1)}), bf16[16,2,2048]{2,1,0:T(2,128)(2,1)S(1)}, u32[]{:S(2)}, u32[]{:S(2)}) async-start(bf16[16,2,2048]{2,1,0:T(2,128)(2,1)} %reshape.271), calls=%async_computation.3 | async-start | bytes 262144 | tf_op jit(solution)/shard_map/all_to_all | solution.py:16
Sparse Core Ops, SparseCore 0:
  34.7 66.9 reduce-scatter.1

commit v4 on v3

--- a/solution.py
+++ b/solution.py
@@ -10,13 +10,17 @@
 
 def tp_sum(part):
     width = lax.axis_size("tp")
-    chunks = part.reshape(width, -1)
+    seats, tokens, rank = part.shape
+    lanes = part.reshape(seats // 2, 2, tokens, rank).transpose(2, 0, 1, 3)
+    lanes = lanes.reshape(tokens, seats // 2, 2 * rank)
+    chunks = lanes.reshape(width, -1, 2 * rank)
     gathered = lax.all_to_all(chunks, "tp", split_axis=0, concat_axis=0, tiled=True)
     summed = jnp.sum(gathered.astype(jnp.float32), axis=0, keepdims=True).astype(jnp.bfloat16)
     spread = lax.all_to_all(
         jnp.broadcast_to(summed, chunks.shape), "tp", split_axis=0, concat_axis=0, tiled=True
     )
-    return spread.reshape(part.shape)
+    spread = spread.reshape(tokens, seats // 2, 2, rank).transpose(1, 2, 0, 3)
+    return spread.reshape(seats, tokens, rank)
 
 
 def shards(

time: 127 us -> 124 us (0.976); the launches traced: 127 us -> 122 us
  other arithmetic: 7.26 us -> 4.59 us
  local copies, waits for them, and re-layouts: 8.53 us -> 6.97 us
  waiting for transfers between devices: 30.5 us -> 29.1 us
    all_to_all x1, blocking collectives: 20.1 us -> 21.8 us  [shards(): lax.all_to_all(seat_delta.reshape(replicas, capacity, per_row, output_col...]
    broadcast_in_dim x1 -> x0, other arithmetic: 1.42 us -> none  [tp_sum(): jnp.broadcast_to(summed, chunks.shape)]
    all_to_all x1, waiting for transfers between devices: 9.56 us -> 8.21 us  [tp_sum(): lax.all_to_all(jnp.broadcast_to(summed, chunks.shape), 'tp', split_axis=0...]
  transfers between devices with their start and end apart: 3 -> 3, of which waited for: 2 -> 2; matrix products, arithmetic and copies ran while one was open for 11% -> 8% of each run, Pallas kernels for 0% -> 0%
where the time goes in v4:
time: 124 us; the launch traced here: 122 us
  blocking collectives  42.6 us (34%)
  waiting for transfers between devices  29.1 us (23%)
  starting transfers between devices  17.2 us (14%)
  between operations  13.7 us (11%)
  matrix products  8.08 us (7%)
  local copies, waits for them, and re-layouts  6.97 us (6%)
  other arithmetic  4.59 us (4%)
    all_to_all x1, blocking collectives, shards(): lax.all_to_all(seat_delta.reshape(replicas, capacity, per_row, output_col...  21.8 us
    all_to_all x1, waiting for transfers between devices, shards(): lax.all_to_all(payload, 'rep', split_axis=0, concat_axis=0, tiled=True)  20.9 us
    all_to_all x1, blocking collectives, tp_sum(): lax.all_to_all(chunks, 'tp', split_axis=0, concat_axis=0, tiled=True)  20.8 us
    all_to_all x1, starting transfers between devices, shards(): lax.all_to_all(payload, 'rep', split_axis=0, concat_axis=0, tiled=True)  13.7 us
    all_to_all x1, waiting for transfers between devices, tp_sum(): lax.all_to_all(jnp.broadcast_to(summed, chunks.shape), 'tp', split_axis=0...  8.21 us
    dot_general x1, matrix products, shards(): jnp.dot(attended, out_weight, preferred_element_type=jnp.float32)  5.3 us
    all_to_all x1, starting transfers between devices, tp_sum(): lax.all_to_all(jnp.broadcast_to(summed, chunks.shape), 'tp', split_axis=0...  3.41 us
  transfers between devices with their start and end apart: 3, of which 2 were waited for; matrix products, arithmetic and copies ran while one was open for 8% of the time, Pallas kernels for 0%

profile of v4, /device:TPU:1, one launch (start us, length us, event | category | flops | bytes accessed | tf_op | source)
XLA Modules:
  0.0 122.2 jit_solution(15619134776232529754)
XLA Ops:
  6.5 0.8 iota_compare_fusion.3
  7.3 0.7 compare_select_fusion
  8.0 0.1 copy.36
  8.1 0.1 reshape.224
  8.2 1.2 reshape.212
  9.4 0.1 broadcast_compare_fusion
  9.5 0.7 gather_fusion
  10.2 0.4 fusion.36
  10.6 0.3 fusion.4
  10.9 0.3 copy-done.4
  11.3 0.0 copy-done.5
  11.3 0.2 select_reduce_fusion.1
  11.5 0.2 convert_reduce_fusion
  11.7 0.1 select_reduce_fusion
  11.8 0.3 convolution_convert_fusion.2
  12.1 0.2 reshape_reshape_transpose_reshape.3
  12.3 0.6 convolution_convert_fusion.1
  12.9 0.1 broadcast_in_dim.113
  13.0 0.1 pad_maximum_fusion
  13.1 0.5 reshape.214
  13.5 1.8 %copy.39 = bf16[32,2,17,512]{3,1,2,0:T(2,128)(2,1)} copy(bf16[32,2,17,512]{3,1,0,2:T(2,128)(2,1)S(1)} %reshape.214) | data formatting | bytes 2228224 | tf_op jit(solution)/shard_map/reshape | solution.py:108
  15.3 13.7 %all-to-all-start = ((bf16[32,2,17,512]{3,1,2,0:T(2,128)(2,1)}), bf16[32,2,17,512]{3,1,2,0:T(2,128)(2,1)S(1)}, u32[]{:S(2)}, u32[]{:S(2)}) async-start(bf16[32,2,17,512]{3,1,2,0:T(2,128)(2,1)} %copy.39), calls=%async_computation.1 | async-start | bytes 2228224 | tf_op jit(solution)/shard_map/all_to_all | solution.py:111
  29.0 0.0 reduce-scatter.2.cloned.1.call-start
  29.1 0.2 reshape_transpose_reshape.4
  29.3 5.3 %convolution_convert_fusion = bf16[320,4096]{1,0:T(8,128)(2,1)} fusion(bf16[320,512]{1,0:T(8,128)(2,1)S(1)} %reshape_transpose_reshape.4, bf16[512,4096]{1,0:T(8,128)(2,1)} %param.15), kind=kOutput, calls=%fused_computation.2 | convolution fusion | flops 1343488000 | bytes 7143424 | tf_op jit(solution)/shard_map/dot_general | solution.py:84
  34.6 0.0 reduce-scatter.2.cloned.1.call-update
  34.6 0.0 copy-start.3
  34.6 20.9 %all-to-all-done = bf16[32,2,17,512]{3,1,2,0:T(2,128)(2,1)S(1)} async-done(((bf16[32,2,17,512]{3,1,2,0:T(2,128)(2,1)}), bf16[32,2,17,512]{3,1,2,0:T(2,128)(2,1)S(1)}, u32[]{:S(2)}, u32[]{:S(2)}) %all-to-all-start) | async-done | bytes 1114144 | tf_op jit(solution)/shard_map/all_to_all | solution.py:111
  55.5 0.3 copy.40
  55.8 0.1 compare_reduce_fusion.1
  56.0 0.4 convolution_bitcast_fusion.1
  56.5 0.4 fusion.16
  56.9 0.1 reshape.216
  57.1 20.8 %all_to_all.20 = bf16[16,32,128]{2,1,0:T(8,128)(2,1)S(1)} all-to-all(bf16[16,32,128]{2,1,0:T(8,128)(2,1)S(1)} %reshape.216), channel_id=1, replica_groups=mesh['rep'=32,'tp'=16] {'tp'}, dimensions={0} | all-to-all | bytes 262144 | tf_op jit(solution)/shard_map/all_to_all | solution.py:17
  77.9 0.7 broadcast_in_dim.118
  78.6 3.4 %all-to-all-start.2 = ((bf16[16,32,128]{2,1,0:T(8,128)(2,1)}), bf16[16,32,128]{2,1,0:T(8,128)(2,1)S(1)}, u32[]{:S(2)}, u32[]{:S(2)}) async-start(bf16[16,32,128]{2,1,0:T(8,128)(2,1)} %broadcast_in_dim.118), calls=%async_computation.3 | async-start | bytes 262144 | tf_op jit(solution)/shard_map/all_to_all | solution.py:19
  82.0 0.2 compare_reduce_fusion
  82.2 8.2 %all-to-all-done.2 = bf16[16,32,128]{2,1,0:T(8,128)(2,1)S(1)} async-done(((bf16[16,32,128]{2,1,0:T(8,128)(2,1)}), bf16[16,32,128]{2,1,0:T(8,128)(2,1)S(1)}, u32[]{:S(2)}, u32[]{:S(2)}) %all-to-all-start.2) | async-done | bytes 131104 | tf_op jit(solution)/shard_map/all_to_all | solution.py:19
  90.4 0.1 reshape.217
  90.6 0.3 copy.43
  90.9 0.4 convolution_bitcast_fusion
  91.3 0.1 fusion.34
  91.4 0.1 select_convert_fusion
  91.5 21.8 %all_to_all.21 = bf16[32,2,16,256]{3,2,1,0:T(8,128)(2,1)S(1)} all-to-all(bf16[32,2,16,256]{3,2,1,0:T(8,128)(2,1)S(1)} %select_convert_fusion), channel_id=1, replica_groups=mesh['rep'=32,'tp'=16] {'rep'}, dimensions={0} | all-to-all | bytes 1048576 | tf_op jit(solution)/shard_map/all_to_all | solution.py:126
  113.3 0.3 convolution_multiply_fusion.1
  113.5 0.1 copy.45
  113.7 0.0 reduce-scatter.2.cloned.1.call-done
  113.7 1.6 %fusion.14 = bf16[320,256]{1,0:T(8,128)(2,1)} fusion(f32[20,16,256]{2,1,0:T(8,128)S(1)} %copy.45, bf16[320,256]{1,0:T(8,128)(2,1)} %reduce-scatter.2.cloned.1.call-done), kind=kLoop, calls=%fused_computation.29 | loop fusion | flops 245760 | bytes 655360 | tf_op jit(solution)/shard_map/convert_element_type | solution.py:139
  (19 shorter events, 0.2 us)
Async XLA Ops:
  6.5 2.9 %copy-start = (bf16[44,1,8,256]{3,2,1,0:T(8,128)(2,1)S(1)}, bf16[44,1,8,256]{3,2,1,0:T(8,128)(2,1)}, u32[]{:S(2)}) copy-start(bf16[44,1,8,256]{3,2,1,0:T(8,128)(2,1)} %param.12) | copy-start | bytes 540676
  6.5 3.6 %copy-start.2 = (bf16[320,256]{1,0:T(8,128)(2,1)S(1)}, bf16[320,256]{1,0:T(8,128)(2,1)}, u32[]{:S(2)}) copy-start(bf16[320,256]{1,0:T(8,128)(2,1)} %param.11) | copy-start | bytes 491524
  10.6 0.7 copy-start.4
  10.6 0.7 copy-start.5
  15.3 40.2 %all-to-all-start = ((bf16[32,2,17,512]{3,1,2,0:T(2,128)(2,1)}), bf16[32,2,17,512]{3,1,2,0:T(2,128)(2,1)S(1)}, u32[]{:S(2)}, u32[]{:S(2)}) async-start(bf16[32,2,17,512]{3,1,2,0:T(2,128)(2,1)} %copy.39), calls=%async_computation.1 | async-start | bytes 2228224 | tf_op jit(solution)/shard_map/all_to_all | solution.py:111
  29.0 84.6 %reduce-scatter.2.cloned.1.call-start = ((), (), s32[]{:S(2)}) async-start(), calls=%async_computation.5 | async-start | bytes 2785280 | tf_op jit(solution)/shard_map/reduce_scatter | solution.py:83
  34.6 21.4 %copy-start.3 = (bf16[2,64,512]{2,1,0:T(8,128)(2,1)S(1)}, bf16[2,64,512]{2,1,0:T(8,128)(2,1)}, u32[]{:S(2)}) copy-start(bf16[2,64,512]{2,1,0:T(8,128)(2,1)} %param.16) | copy-start | bytes 393220
  56.5 34.4 %copy-start.1 = (bf16[2,64,256]{2,1,0:T(8,128)(2,1)S(1)}, bf16[2,64,256]{2,1,0:T(8,128)(2,1)}, u32[]{:S(2)}) copy-start(bf16[2,64,256]{2,1,0:T(8,128)(2,1)} %param.17) | copy-start | bytes 196612
  78.6 11.9 %all-to-all-start.2 = ((bf16[16,32,128]{2,1,0:T(8,128)(2,1)}), bf16[16,32,128]{2,1,0:T(8,128)(2,1)S(1)}, u32[]{:S(2)}, u32[]{:S(2)}) async-start(bf16[16,32,128]{2,1,0:T(8,128)(2,1)} %broadcast_in_dim.118), calls=%async_computation.3 | async-start | bytes 262144 | tf_op jit(solution)/shard_map/all_to_all | solution.py:19
Sparse Core Ops, SparseCore 0:
  34.7 65.2 reduce-scatter.1
